TPU v7x, 512 devices: a whole 4x4x16 slice. The times are simulated.
512 devices in a mesh: ctx: 64 (over x, z_lo, core), head: 8 (over y, z_hi).
Axes of the slice: x: 4, y: 4, z: 16 (z_hi: 2, z_lo: 8; z = z_hi * 8 + z_lo), core: 2. Of those that a mesh axis runs over, the one named last changes fastest.
Arguments:
- queries: bfloat16 [16384, 2048], P('ctx', 'head'), may hold values from -40 to 40
- keys: bfloat16 [16384, 2048], P('ctx', 'head'), may hold values from -4 to 4
- values: bfloat16 [16384, 2048], P('ctx', 'head'), may hold values from -5 to 5
- selected: int32 [16, 512, 3], P('head', 'ctx'), may hold values from 0 to 63, as said below
- out_weight: bfloat16 [2048, 2048], P(None, 'head'), may hold values from -0.125 to 0.125
Outputs:
- projected: bfloat16 [16384, 2048], P('ctx', 'head')
Inputs may be any that keep to these rules, and one draw needn't show every extreme that they name: `selected`: entry 0 of a tile's selection is its own block; entries 1 and 2 are two different earlier blocks, or both the own block where no earlier block is chosen for the tile (one earlier block and the own block in the second key block). For each head, the tiles of one key block name any one other block at most 2 times, and exactly 2 times for every block they name, from the third key block on.
All inputs are finite; a program needn't handle non-finite values.
Results may differ from a plain program's by a relative error of at most 0.0054.
Values may be sent and summed in bfloat16 or wider, within the bound.
No kernel may reach another device: no remote copies, remote signals or barrier semaphores. Data moves between devices by JAX's collectives and lax.ppermute only.
A program may use at most 64 MiB of HBM per device.

v0:
```python
import math
import jax
import jax.numpy as jnp
from jax import lax
from jax.sharding import PartitionSpec as P

CAP = 2


def owner_block(group, keys_three, vals_three, scale):
    scores = (
        jnp.einsum("gchtd,khd->gchtk", group, keys_three, preferred_element_type=jnp.float32)
        * scale
    )
    top = jnp.max(scores, axis=-1)
    prob = jnp.exp(scores - top[..., None])
    total = jnp.sum(prob, axis=-1)
    part = jnp.einsum(
        "gchtk,khd->gchtd",
        prob.astype(jnp.bfloat16),
        vals_three,
        preferred_element_type=jnp.float32,
    )
    return (part / total[..., None], top + jnp.log(total))


def partials_back(outputs, sums):
    return (
        lax.all_to_all(outputs, "ctx", split_axis=0, concat_axis=0, tiled=True),
        lax.all_to_all(sums, "ctx", split_axis=0, concat_axis=0, tiled=True),
    )


def group_size(sources, rows_each):
    size = max(1, 512 // rows_each)
    size = min(size, sources)
    while sources % size != 0:
        size = size - 1
    return size


def local(queries, keys, values, selected, out_weight):
    heads_loc = selected.shape[0]
    tiles = selected.shape[1]
    tokens_here = queries.shape[0]
    width = queries.shape[1] // heads_loc
    tile_rows = tokens_here // tiles
    sources = lax.axis_size("ctx")
    mine = lax.axis_index("ctx")
    scale = width ** (-0.5)
    quer_three = queries.reshape(tokens_here, heads_loc, width)
    keys_three = keys.reshape(tokens_here, heads_loc, width)
    vals_three = values.reshape(tokens_here, heads_loc, width)
    rows_blk = math.gcd(tokens_here, 512)
    row_groups = tokens_here // rows_blk
    key_pos = jnp.arange(tokens_here, dtype=jnp.int32)

    def own_rows(args):
        query_rows, start = args
        scores = (
            jnp.einsum("rhd,khd->hrk", query_rows, keys_three, preferred_element_type=jnp.float32)
            * scale
        )
        allowed = (start + jnp.arange(rows_blk, dtype=jnp.int32))[:, None] >= key_pos[None, :]
        scores = jnp.where(allowed[None], scores, jnp.float32(-1e30))
        top = jnp.max(scores, axis=-1)
        prob = jnp.exp(scores - top[..., None])
        total = jnp.sum(prob, axis=-1)
        part = jnp.einsum(
            "hrk,khd->hrd",
            prob.astype(jnp.bfloat16),
            vals_three,
            preferred_element_type=jnp.float32,
        )
        return (part / total[..., None], top + jnp.log(total))

    own_out, own_lse = lax.map(
        own_rows,
        (
            quer_three.reshape(row_groups, rows_blk, heads_loc, width),
            jnp.arange(row_groups, dtype=jnp.int32) * rows_blk,
        ),
    )
    own_out = jnp.transpose(own_out, (1, 0, 2, 3)).reshape(heads_loc, tiles, tile_rows, width)
    own_lse = jnp.transpose(own_lse, (1, 0, 2)).reshape(heads_loc, tiles, tile_rows)
    picks = selected[:, :, 1:]
    valid = picks != mine
    target = jnp.where(valid, picks, sources)
    onehot = (target[..., None] == jnp.arange(sources, dtype=jnp.int32)).astype(jnp.int32)
    flat_hot = onehot.reshape(heads_loc, tiles * 2, sources)
    before = jnp.cumsum(flat_hot, axis=1) - flat_hot
    slot = jnp.sum(before * flat_hot, axis=-1).reshape(heads_loc, tiles, 2)
    head_idx = jnp.broadcast_to(
        jnp.arange(heads_loc, dtype=jnp.int32)[:, None, None], (heads_loc, tiles, 2)
    )
    query_src = jnp.transpose(quer_three.reshape(tiles, tile_rows, heads_loc, width), (2, 0, 1, 3))
    query_pairs = jnp.broadcast_to(query_src[:, :, None], (heads_loc, tiles, 2, tile_rows, width))
    send_q = jnp.zeros((sources, CAP, heads_loc, tile_rows, width), jnp.bfloat16)
    send_q = send_q.at[target, slot, head_idx].set(query_pairs, mode="drop")
    got_rows = lax.all_to_all(send_q, "ctx", split_axis=0, concat_axis=0, tiled=True)
    count = got_rows.shape[1]
    group_count = group_size(sources, count * heads_loc * tile_rows)
    query_groups = got_rows.reshape(
        sources // group_count, group_count, count, heads_loc, tile_rows, width
    )

    def one_group(group):
        return owner_block(group, keys_three, vals_three, scale)

    outputs, sums = lax.map(one_group, query_groups)
    got_out, got_lse = partials_back(
        outputs.reshape(sources, count, heads_loc, tile_rows, width),
        sums.reshape(sources, count, heads_loc, tile_rows),
    )
    clipped = jnp.clip(target, 0, sources - 1)
    pick_out = got_out[clipped, slot, head_idx]
    pick_lse = got_lse[clipped, slot, head_idx]
    keep = valid[..., None]
    top = jnp.maximum(own_lse, jnp.max(jnp.where(keep, pick_lse, own_lse[:, :, None]), axis=2))
    own_w = jnp.exp(own_lse - top)
    pick_w = jnp.exp(jnp.where(keep, pick_lse - top[:, :, None], jnp.float32(-1e30)))
    numer = own_w[..., None] * own_out + jnp.sum(pick_w[..., None] * pick_out, axis=2)
    denom = own_w + jnp.sum(pick_w, axis=2)
    attention = jnp.transpose(numer / denom[..., None], (1, 2, 0, 3)).reshape(
        tokens_here, heads_loc * width
    )
    attention = attention.astype(jnp.bfloat16)
    projected = jnp.dot(
        lax.all_gather(attention, "head", axis=1, tiled=True),
        out_weight,
        preferred_element_type=jnp.float32,
    )
    return projected.astype(jnp.bfloat16)


def solution(mesh):
    return jax.shard_map(
        local,
        mesh=mesh,
        in_specs=(
            P("ctx", "head"),
            P("ctx", "head"),
            P("ctx", "head"),
            P("head", "ctx", None),
            P(None, "head"),
        ),
        out_specs=P("ctx", "head"),
        check_vma=False,
    )
```

profile of v0, /device:TPU:2, one launch (start us, length us, event | category | flops | bytes accessed | tf_op | source)
XLA Modules:
  0.0 489.7 jit_solution(11999929789895695316)
XLA Ops:
  6.5 0.8 fusion.23
  8.2 0.9 reshape_reshape.4
  9.2 1.9 broadcast_in_dim.120
  11.1 4.2 scatter_fusion
  15.2 16.1 %all-to-all-start = ((bf16[64,2,2,32,128]{4,3,2,1,0:T(8,128)(2,1)}), bf16[64,2,2,32,128]{4,3,2,1,0:T(8,128)(2,1)S(1)}, u32[]{:S(2)}, u32[]{:S(2)}) async-start(bf16[64,2,2,32,128]{4,3,2,1,0:T(8,128)(2,1)} %scatter_fusion), calls=%async_computation | async-start | bytes 4194304 | tf_op jit(solution)/shard_map/all_to_all | solution.py:100
  31.6 1.0 copy.55
  32.6 0.7 copy.58
  33.3 92.5 %all-to-all-done = bf16[64,2,2,32,128]{4,3,2,1,0:T(8,128)(2,1)S(1)} async-done(((bf16[64,2,2,32,128]{4,3,2,1,0:T(8,128)(2,1)}), bf16[64,2,2,32,128]{4,3,2,1,0:T(8,128)(2,1)S(1)}, u32[]{:S(2)}, u32[]{:S(2)}) %all-to-all-start) | async-done | bytes 2097184 | tf_op jit(solution)/shard_map/all_to_all | solution.py:100
  125.9 50.5 %while.2 = (s32[]{:T(128)}, f32[16,4,2,2,32,128]{5,4,3,2,1,0:T(8,128)}, f32[16,4,2,2,32]{4,3,2,1,0:T(2,128)}, bf16[16,4,2,2,32,128]{5,4,3,2,1,0:T(8,128)(2,1)S(1...) while((s32[]{:T(128)}, f32[16,4,2,2,32,128]{5,4,3,2,1,0:T(8,128)}, ...), condition=%wide.region_8.9_spmd, body=%wide.region_5.8_spmd.sunk | while | flops 67960320 | bytes 2779233 | solution.py:110
  126.5 1.2 fusion.42
  129.6 1.2 fusion.42
  132.8 1.2 fusion.42
  135.9 1.2 fusion.42
  139.1 1.2 fusion.42
  142.2 1.2 fusion.42
  145.4 1.2 fusion.42
  148.6 1.2 fusion.42
  151.7 1.2 fusion.42
  154.9 1.2 fusion.42
  158.0 1.2 fusion.42
  161.2 1.2 fusion.42
  164.4 1.2 fusion.42
  167.5 1.2 fusion.42
  170.7 1.2 fusion.42
  173.8 1.2 fusion.42
  176.4 1.1 reshape.180
  177.5 21.2 %all_to_all.15 = f32[64,1,128]{2,1,0:T(1,128)S(1)} all-to-all(f32[64,1,128]{2,1,0:T(1,128)S(1)} %reshape.180), channel_id=1, replica_groups=mesh['ctx'=64,'head'=8] {'ctx'}, dimensions={0} | all-to-all | bytes 65536 | tf_op jit(solution)/shard_map/all_to_all | solution.py:30
  198.6 6.6 %all-to-all-start.2 = ((f32[64,2,2,32,128]{4,3,2,1,0:T(8,128)}), f32[64,2,2,32,128]{4,3,2,1,0:T(8,128)}, u32[]{:S(2)}, u32[]{:S(2)}) async-start(f32[64,2,2,32,128]{4,3,2,1,0:T(8,128)} %bitcast.87), calls=%async_computation.2 | async-start | bytes 8388608 | tf_op jit(solution)/shard_map/all_to_all | solution.py:29
  208.8 178.8 %all-to-all-done.2 = f32[64,2,2,32,128]{4,3,2,1,0:T(8,128)} async-done(((f32[64,2,2,32,128]{4,3,2,1,0:T(8,128)}), f32[64,2,2,32,128]{4,3,2,1,0:T(8,128)}, u32[]{:S(2)}, u32[]{:S(2)}) %all-to-all-start.2) | async-done | bytes 4194336 | tf_op jit(solution)/shard_map/all_to_all | solution.py:29
  387.6 2.8 gather_fusion.1
  391.7 88.8 %all-gather.2.cloned.1.call-done = bf16[256,2048]{1,0:T(8,128)(2,1)} async-done(((bf16[256,256]{1,0:T(8,128)(2,1)}), bf16[256,2048]{1,0:T(8,128)(2,1)}) %all-gather.2.cloned.1.call-update) | async-done | bytes 1048592 | tf_op jit(solution)/shard_map/all_gather | solution.py:129
  480.5 2.3 convolution_convert_fusion
  (126 shorter events, 36.9 us)
Async XLA Ops:
  6.5 474.0 %copy-start = (bf16[2048,256]{1,0:T(8,128)(2,1)S(1)}, bf16[2048,256]{1,0:T(8,128)(2,1)}, u32[]{:S(2)}) copy-start(bf16[2048,256]{1,0:T(8,128)(2,1)} %param.11) | copy-start | bytes 3145732
  6.5 24.8 %copy-start.2 = (bf16[256,256]{1,0:T(8,128)(2,1)S(1)}, bf16[256,256]{1,0:T(8,128)(2,1)}, u32[]{:S(2)}) copy-start(bf16[256,256]{1,0:T(8,128)(2,1)} %param.8) | copy-start | bytes 393220
  15.2 110.6 %all-to-all-start = ((bf16[64,2,2,32,128]{4,3,2,1,0:T(8,128)(2,1)}), bf16[64,2,2,32,128]{4,3,2,1,0:T(8,128)(2,1)S(1)}, u32[]{:S(2)}, u32[]{:S(2)}) async-start(bf16[64,2,2,32,128]{4,3,2,1,0:T(8,128)(2,1)} %scatter_fusion), calls=%async_computation | async-start | bytes 4194304 | tf_op jit(solution)/shard_map/all_to_all | solution.py:100
  198.6 7.0 %copy-start.1 = (bf16[256,256]{1,0:T(8,128)(2,1)S(1)}, bf16[256,256]{1,0:T(8,128)(2,1)}, u32[]{:S(2)}) copy-start(bf16[256,256]{1,0:T(8,128)(2,1)} %param.7) | copy-start | bytes 393220
  198.6 189.0 %all-to-all-start.2 = ((f32[64,2,2,32,128]{4,3,2,1,0:T(8,128)}), f32[64,2,2,32,128]{4,3,2,1,0:T(8,128)}, u32[]{:S(2)}, u32[]{:S(2)}) async-start(f32[64,2,2,32,128]{4,3,2,1,0:T(8,128)} %bitcast.87), calls=%async_computation.2 | async-start | bytes 8388608 | tf_op jit(solution)/shard_map/all_to_all | solution.py:29
  205.2 275.3 %all-gather.2.cloned.1.call-start = ((), (), s32[]{:S(2)}) async-start(), calls=%async_computation.3 | async-start | bytes 1179648 | tf_op jit(solution)/shard_map/all_gather | solution.py:129
Sparse Core Ops, SparseCore 0:
  391.8 88.6 all-gather.1
where the time goes:
time: 491 us; the launch traced here: 490 us
  waiting for transfers between devices  360 us (73%)
  local copies, waits for them, and re-layouts  37.3 us (8%)
  matrix products  26.9 us (5%)
  starting transfers between devices  22.7 us (5%)
  blocking collectives  21.2 us (4%)
  between operations  13.6 us (3%)
  other arithmetic  7.41 us (2%)
    all_to_all x1, waiting for transfers between devices, partials_back(): lax.all_to_all(outputs, 'ctx', split_axis=0, concat_axis=0, tiled=True)  179 us
    all_to_all x1, waiting for transfers between devices, local(): lax.all_to_all(send_q, 'ctx', split_axis=0, concat_axis=0, tiled=True)  92.5 us
    all_gather x1, waiting for transfers between devices, local(): lax.all_gather(attention, 'head', axis=1, tiled=True)  88.8 us
    dynamic_update_slice x32, local copies, waits for them, and re-layouts, local(): outputs, sums = lax.map(one_group, query_groups)  21.3 us
    all_to_all x1, blocking collectives, partials_back(): lax.all_to_all(sums, 'ctx', split_axis=0, concat_axis=0, tiled=True)  21.2 us
    dot_general x16, matrix products, owner_block(): jnp.einsum('gchtk,khd->gchtd', prob.astype(jnp.bfloat16), vals_three, pre...  19.1 us
    all_to_all x1, starting transfers between devices, local(): lax.all_to_all(send_q, 'ctx', split_axis=0, concat_axis=0, tiled=True)  16.1 us
  transfers between devices with their start and end apart: 3, of which 3 were waited for; matrix products, arithmetic and copies ran while one was open for 1% of the time, Pallas kernels for 0%

commit v1 on v0

--- a/solution.py
+++ b/solution.py
@@ -126,7 +126,9 @@
     )
     attention = attention.astype(jnp.bfloat16)
     projected = jnp.dot(
-        lax.all_gather(attention, "head", axis=1, tiled=True),
+        jnp.concatenate(
+            lax.all_to_all(jnp.stack([attention] * lax.axis_size("head")), "head", 0, 0), axis=1
+        ),
         out_weight,
         preferred_element_type=jnp.float32,
     )

time: 491 us -> 452 us (0.921)
  the two profiles are of different devices: /device:TPU:2 before, /device:TPU:7 now
where the time goes in v1:
time: 452 us
  waiting for transfers between devices  276 us (61%)
  blocking collectives  80.6 us (18%)
  local copies, waits for them, and re-layouts  36.8 us (8%)
  matrix products  25.8 us (6%)
  starting transfers between devices  24.4 us (5%)
  other arithmetic  7.41 us (2%)
    all_to_all x1, waiting for transfers between devices, partials_back(): lax.all_to_all(outputs, 'ctx', split_axis=0, concat_axis=0, tiled=True)  182 us
    all_to_all x1, waiting for transfers between devices, local(): lax.all_to_all(send_q, 'ctx', split_axis=0, concat_axis=0, tiled=True)  93.8 us
    all_to_all x1, blocking collectives, local(): lax.all_to_all(jnp.stack([attention] * lax.axis_size('head')), 'head', 0, 0)  62 us
    dynamic_update_slice x32, local copies, waits for them, and re-layouts, local(): outputs, sums = lax.map(one_group, query_groups)  21.3 us
    dot_general x16, matrix products, owner_block(): jnp.einsum('gchtk,khd->gchtd', prob.astype(jnp.bfloat16), vals_three, pre...  19 us
    all_to_all x1, blocking collectives, partials_back(): lax.all_to_all(sums, 'ctx', split_axis=0, concat_axis=0, tiled=True)  18.6 us
    all_to_all x1, starting transfers between devices, local(): lax.all_to_all(send_q, 'ctx', split_axis=0, concat_axis=0, tiled=True)  16.5 us
  transfers between devices with their start and end apart: 2, of which 2 were waited for; matrix products, arithmetic and copies ran while one was open for 1% of the time, Pallas kernels for 0%

profile of v1, /device:TPU:7, one launch (start us, length us, event | category | flops | bytes accessed | tf_op | source)
XLA Modules:
  0.0 451.6 jit_solution(241048697076032231)
XLA Ops:
  0.0 0.8 fusion.23
  1.6 0.9 reshape_reshape.4
  2.7 1.9 broadcast_in_dim.120
  4.5 4.2 scatter_fusion
  8.7 16.5 %all-to-all-start = ((bf16[64,2,2,32,128]{4,3,2,1,0:T(8,128)(2,1)}), bf16[64,2,2,32,128]{4,3,2,1,0:T(8,128)(2,1)S(1)}, u32[]{:S(2)}, u32[]{:S(2)}) async-start(bf16[64,2,2,32,128]{4,3,2,1,0:T(8,128)(2,1)} %scatter_fusion), calls=%async_computation | async-start | bytes 4194304 | tf_op jit(solution)/shard_map/all_to_all | solution.py:100
  25.5 1.0 copy.56
  26.5 0.7 copy.59
  27.2 93.8 %all-to-all-done = bf16[64,2,2,32,128]{4,3,2,1,0:T(8,128)(2,1)S(1)} async-done(((bf16[64,2,2,32,128]{4,3,2,1,0:T(8,128)(2,1)}), bf16[64,2,2,32,128]{4,3,2,1,0:T(8,128)(2,1)S(1)}, u32[]{:S(2)}, u32[]{:S(2)}) %all-to-all-start) | async-done | bytes 2097184 | tf_op jit(solution)/shard_map/all_to_all | solution.py:100
  121.0 50.5 %while.2 = (s32[]{:T(128)}, f32[16,4,2,2,32,128]{5,4,3,2,1,0:T(8,128)}, f32[16,4,2,2,32]{4,3,2,1,0:T(2,128)}, bf16[16,4,2,2,32,128]{5,4,3,2,1,0:T(8,128)(2,1)S(1...) while((s32[]{:T(128)}, f32[16,4,2,2,32,128]{5,4,3,2,1,0:T(8,128)}, ...), condition=%wide.region_8.9_spmd, body=%wide.region_5.8_spmd.sunk | while | flops 67960320 | bytes 2779233 | solution.py:110
  121.6 1.2 fusion.42
  124.8 1.2 fusion.42
  127.9 1.2 fusion.42
  131.1 1.2 fusion.42
  134.2 1.2 fusion.42
  137.4 1.2 fusion.42
  140.6 1.2 fusion.42
  143.7 1.2 fusion.42
  146.9 1.2 fusion.42
  150.0 1.2 fusion.42
  153.2 1.2 fusion.42
  156.3 1.2 fusion.42
  159.5 1.2 fusion.42
  162.7 1.2 fusion.42
  165.8 1.2 fusion.42
  169.0 1.2 fusion.42
  171.5 1.1 reshape.191
  172.6 18.6 %all_to_all.20 = f32[64,1,128]{2,1,0:T(1,128)S(1)} all-to-all(f32[64,1,128]{2,1,0:T(1,128)S(1)} %reshape.191), channel_id=1, replica_groups=mesh['ctx'=64,'head'=8] {'ctx'}, dimensions={0} | all-to-all | bytes 65536 | tf_op jit(solution)/shard_map/all_to_all | solution.py:30
  191.2 7.9 %all-to-all-start.2 = ((f32[64,2,2,32,128]{4,3,2,1,0:T(8,128)}), f32[64,2,2,32,128]{4,3,2,1,0:T(8,128)}, u32[]{:S(2)}, u32[]{:S(2)}) async-start(f32[64,2,2,32,128]{4,3,2,1,0:T(8,128)} %bitcast.90), calls=%async_computation.2 | async-start | bytes 8388608 | tf_op jit(solution)/shard_map/all_to_all | solution.py:29
  202.6 182.2 %all-to-all-done.2 = f32[64,2,2,32,128]{4,3,2,1,0:T(8,128)} async-done(((f32[64,2,2,32,128]{4,3,2,1,0:T(8,128)}), f32[64,2,2,32,128]{4,3,2,1,0:T(8,128)}, u32[]{:S(2)}, u32[]{:S(2)}) %all-to-all-start.2) | async-done | bytes 4194336 | tf_op jit(solution)/shard_map/all_to_all | solution.py:29
  384.8 2.8 gather_fusion.1
  388.5 62.0 %all_to_all.21 = bf16[8,256,256]{1,2,0:T(8,128)(2,1)S(1)} all-to-all(bf16[8,256,256]{1,2,0:T(8,128)(2,1)S(1)} %stack.2), channel_id=1, replica_groups=mesh['ctx'=64,'head'=8] {'head'}, dimensions={0} | all-to-all | bytes 2097152 | tf_op jit(solution)/shard_map/all_to_all | solution.py:130
  450.4 1.1 convolution_convert_fusion
  (126 shorter events, 36.4 us)
Async XLA Ops:
  0.0 450.4 %copy-start = (bf16[2048,256]{1,0:T(8,128)(2,1)S(1)}, bf16[2048,256]{1,0:T(8,128)(2,1)}, u32[]{:S(2)}) copy-start(bf16[2048,256]{1,0:T(8,128)(2,1)} %param.11) | copy-start | bytes 3145732
  0.0 25.2 %copy-start.2 = (bf16[256,256]{1,0:T(8,128)(2,1)S(1)}, bf16[256,256]{1,0:T(8,128)(2,1)}, u32[]{:S(2)}) copy-start(bf16[256,256]{1,0:T(8,128)(2,1)} %param.8) | copy-start | bytes 393220
  8.7 112.3 %all-to-all-start = ((bf16[64,2,2,32,128]{4,3,2,1,0:T(8,128)(2,1)}), bf16[64,2,2,32,128]{4,3,2,1,0:T(8,128)(2,1)S(1)}, u32[]{:S(2)}, u32[]{:S(2)}) async-start(bf16[64,2,2,32,128]{4,3,2,1,0:T(8,128)(2,1)} %scatter_fusion), calls=%async_computation | async-start | bytes 4194304 | tf_op jit(solution)/shard_map/all_to_all | solution.py:100
  191.2 8.3 %copy-start.1 = (bf16[256,256]{1,0:T(8,128)(2,1)S(1)}, bf16[256,256]{1,0:T(8,128)(2,1)}, u32[]{:S(2)}) copy-start(bf16[256,256]{1,0:T(8,128)(2,1)} %param.7) | copy-start | bytes 393220
  191.2 193.6 %all-to-all-start.2 = ((f32[64,2,2,32,128]{4,3,2,1,0:T(8,128)}), f32[64,2,2,32,128]{4,3,2,1,0:T(8,128)}, u32[]{:S(2)}, u32[]{:S(2)}) async-start(f32[64,2,2,32,128]{4,3,2,1,0:T(8,128)} %bitcast.90), calls=%async_computation.2 | async-start | bytes 8388608 | tf_op jit(solution)/shard_map/all_to_all | solution.py:29
